TPU v7x, 128 devices: a whole 4x4x4 slice. The times are simulated.
128 devices in a mesh: dp: 8 (over y, core), tensor: 16 (over z, x).
Axes of the slice: x: 4, y: 4, z: 4, core: 2. Of those that a mesh axis runs over, the one named last changes fastest.
Arguments:
- features: bfloat16 [1024, 4096], P('dp'), may hold values from -6 to 6
- enc_in: bfloat16 [4096, 2048], P(None, 'tensor'), may hold values from -0.09375 to 0.09375
- enc_out: bfloat16 [2048, 8192], P('tensor'), may hold values from -0.125 to 0.125
- noise: bfloat16 [1024, 4096], P('dp', 'tensor'), may hold values from -6 to 6
- in_weight: bfloat16 [4096, 16384], P('dp', 'tensor'), may hold values from -0.09375 to 0.09375
- out_weight: bfloat16 [4096, 16384], P('dp', 'tensor'), may hold values from -0.046875 to 0.046875
- probes: bfloat16 [2, 1024, 4096], P(None, 'dp'), may hold values from -6 to 6
Outputs:
- flowed: float32 [1024, 4096], P('dp', 'tensor')
- logdet: float32 [1024], P('dp')
All inputs are finite; a program needn't handle non-finite values.
Results may differ from a plain program's by a relative error of at most 0.017.
Values may be sent and summed in bfloat16 or wider, within the bound.
No kernel may reach another device: no remote copies, remote signals or barrier semaphores. Data moves between devices by JAX's collectives and lax.ppermute only.
A program may use at most 128 MiB of HBM per device.

v0:
```python
import jax
import jax.numpy as jnp
from jax import lax
from jax.sharding import PartitionSpec as P

L = 4096
PROBES = 2
TERMS = 3


def collect(partial_value):
    return lax.psum(partial_value.astype(jnp.bfloat16), "tensor")


def series(start, w_in, w_out, slope):
    start32 = start.astype(jnp.float32)
    current = start
    running = jnp.zeros((start.shape[1],), jnp.float32)
    for term_idx in range(TERMS):
        pulled = jnp.einsum("pbl,lh->pbh", current, w_out, preferred_element_type=jnp.float32)
        scaled = (pulled * slope[None]).astype(jnp.bfloat16)
        partial_value = jnp.einsum("pbh,lh->pbl", scaled, w_in, preferred_element_type=jnp.float32)
        current = collect(partial_value)
        coeff = (-1.0) ** term_idx / (term_idx + 1)
        running = running + coeff * jnp.sum(start32 * current.astype(jnp.float32), axis=(0, 2))
    return running


def local(features, enc_in, enc_out, noise, in_weight, out_weight, probes):
    hidden = jax.nn.silu(jnp.dot(features, enc_in, preferred_element_type=jnp.float32)).astype(
        jnp.bfloat16
    )
    partial_stats = jnp.dot(hidden, enc_out, preferred_element_type=jnp.float32)
    batch_rows = partial_stats.shape[0]
    moments = lax.psum_scatter(
        partial_stats.reshape(batch_rows, 2, L), "tensor", scatter_dimension=2, tiled=True
    )
    u_slice = (moments[:, 0] + jax.nn.softplus(moments[:, 1]) * noise.astype(jnp.float32)).astype(
        jnp.bfloat16
    )
    u_full = lax.all_gather(u_slice, "tensor", axis=1, tiled=True)
    w_in, w_out = (
        lax.all_gather(in_weight, "dp", axis=0, tiled=True),
        lax.all_gather(out_weight, "dp", axis=0, tiled=True),
    )
    pre_act = jnp.dot(u_full, w_in, preferred_element_type=jnp.float32)
    tanh_val = jnp.tanh(pre_act)
    squash = tanh_val.astype(jnp.bfloat16)
    slope = 1.0 - tanh_val * tanh_val
    branch_part = jnp.einsum("bh,lh->bl", squash, w_out, preferred_element_type=jnp.float32)
    flowed = u_slice.astype(jnp.float32) + lax.psum_scatter(
        branch_part.astype(jnp.bfloat16), "tensor", scatter_dimension=1, tiled=True
    ).astype(jnp.float32)
    running = series(probes, w_in, w_out, slope)
    logdet = running / PROBES
    return (flowed, logdet)


def solution(mesh):
    in_specs = (
        P("dp", None),
        P(None, "tensor"),
        P("tensor", None),
        P("dp", "tensor"),
        P("dp", "tensor"),
        P("dp", "tensor"),
        P(None, "dp", None),
    )
    out_specs = (P("dp", "tensor"), P("dp"))
    return jax.shard_map(local, mesh=mesh, in_specs=in_specs, out_specs=out_specs, check_vma=False)
```

profile of v0, /device:TPU:0, one launch (start us, length us, event | category | flops | bytes accessed | tf_op | source)
XLA Modules:
  0.0 636.0 jit_solution(1916886400833628591)
XLA Ops:
  7.2 1.5 copy-done
  8.8 4.6 fusion.52
  13.4 4.6 copy.12
  18.0 0.0 all-gather.4.cloned.1.call-start
  18.0 81.1 %reduce-scatter.3.cloned.1.call-done = f32[128,2,256]{2,0,1:T(8,128)} async-done(((f32[128,2,4096]{2,0,1:T(8,128)}), f32[128,2,256]{2,0,1:T(8,128)}) %reduce-scatter.3.cloned.1.call-update) | async-done | bytes 262160 | tf_op jit(solution)/shard_map/reduce_scatter | solution.py:35
  99.1 1.7 fusion.51
  100.9 0.7 all-gather.6.cloned.1.call-update
  101.6 0.5 all-gather.8.cloned.1.call-update
  102.2 42.0 %all-gather.4.cloned.1.call-done = bf16[128,4096]{1,0:T(8,128)(2,1)} async-done(((bf16[128,256]{1,0:T(8,128)(2,1)}), bf16[128,4096]{1,0:T(8,128)(2,1)}) %all-gather.4.cloned.1.call-update) | async-done | bytes 1048592 | tf_op jit(solution)/shard_map/all_gather | solution.py:41
  144.2 50.7 %all-gather.6.cloned.1.call-done = bf16[4096,1024]{1,0:T(8,128)(2,1)} async-done(((bf16[512,1024]{1,0:T(8,128)(2,1)}), bf16[4096,1024]{1,0:T(8,128)(2,1)}) %all-gather.6.cloned.1.call-update) | async-done | bytes 8388624 | tf_op jit(solution)/shard_map/all_gather | solution.py:43
  194.9 5.0 multiply_subtract_fusion
  199.8 46.4 %all-gather.8.cloned.1.call-done = bf16[4096,1024]{1,0:T(8,128)(2,1)} async-done(((bf16[512,1024]{1,0:T(8,128)(2,1)}), bf16[4096,1024]{1,0:T(8,128)(2,1)}) %all-gather.8.cloned.1.call-update) | async-done | bytes 8388624 | tf_op jit(solution)/shard_map/all_gather | solution.py:44
  246.3 12.2 %fusion.12 = bf16[2,128,4096]{2,1,0:T(8,128)(2,1)} fusion(bf16[4096,1024]{1,0:T(8,128)(2,1)} %all-gather.6.cloned.1.call-done, bf16[2,128,4096]{2,1,0:T(8,128)(2,1)} %param.13, bf16[4096,1024]{1,0:T(8,128)(2,1)} %all-gather.8.cloned.1.call-done, f32[128,1024]{1,0:T(8,128)S(1)} %get-tuple-element.5), kind=kOutput, calls=%fused_computation.15 | convolution fusion | flops 4296540160 | bytes 21495808 | tf_op jit(solution)/shard_map/pbh,lh->pbl/dot_general | solution.py:22
  258.5 91.5 %all-reduce.4.cloned.1.call-done = bf16[2,128,4096]{2,1,0:T(8,128)(2,1)} async-done(((bf16[2,128,4096]{2,1,0:T(8,128)(2,1)}), bf16[2,128,4096]{2,1,0:T(8,128)(2,1)}) %all-reduce.4.cloned.1.call-update) | async-done | bytes 2097168 | tf_op jit(solution)/shard_map/psum | solution.py:12
  350.1 12.2 %fusion.15 = bf16[2,128,4096]{2,1,0:T(8,128)(2,1)} fusion(bf16[4096,1024]{1,0:T(8,128)(2,1)} %all-gather.6.cloned.1.call-done, bf16[2,128,4096]{2,1,0:T(8,128)(2,1)} %all-reduce.4.cloned.1.call-done, bf16[4096,1024]{1,0:T(8,128)(2,1)} %all-gather.8.cloned.1.call-done, f32[128,1024]{1,0:T(8,128)S(1)} %get-tuple-element.5), kind=kOutput, calls=%fused_computation.16 | convolution fusion | flops 4296540160 | bytes 21495808 | tf_op jit(solution)/shard_map/pbh,lh->pbl/dot_general | solution.py:22
  362.3 0.2 reduce-scatter.5.cloned.1.call-start
  362.5 7.3 %convolution_convert_fusion = bf16[128,4096]{1,0:T(8,128)(2,1)} fusion(bf16[4096,1024]{1,0:T(8,128)(2,1)} %all-gather.8.cloned.1.call-done, bf16[128,1024]{1,0:T(8,128)(2,1)S(1)} %get-tuple-element.6), kind=kOutput, calls=%fused_computation.18 | convolution fusion | flops 1074266112 | bytes 9699328 | tf_op jit(solution)/shard_map/bh,lh->bl/dot_general | solution.py:50
  369.8 83.3 %all-reduce.6.cloned.1.call-done = bf16[2,128,4096]{2,1,0:T(8,128)(2,1)} async-done(((bf16[2,128,4096]{2,1,0:T(8,128)(2,1)}), bf16[2,128,4096]{2,1,0:T(8,128)(2,1)}) %all-reduce.6.cloned.1.call-update) | async-done | bytes 2097168 | tf_op jit(solution)/shard_map/psum | solution.py:12
  453.1 12.2 %fusion.18 = bf16[2,128,4096]{2,1,0:T(8,128)(2,1)} fusion(bf16[4096,1024]{1,0:T(8,128)(2,1)} %all-gather.6.cloned.1.call-done, bf16[2,128,4096]{2,1,0:T(8,128)(2,1)} %all-reduce.6.cloned.1.call-done, bf16[4096,1024]{1,0:T(8,128)(2,1)} %all-gather.8.cloned.1.call-done, f32[128,1024]{1,0:T(8,128)S(1)} %get-tuple-element.5), kind=kOutput, calls=%fused_computation.17 | convolution fusion | flops 4296540160 | bytes 21495808 | tf_op jit(solution)/shard_map/pbh,lh->pbl/dot_general | solution.py:22
  465.4 64.4 %reduce-scatter.5.cloned.1.call-done = bf16[128,256]{1,0:T(8,128)(2,1)} async-done(((bf16[128,4096]{1,0:T(8,128)(2,1)}), bf16[128,256]{1,0:T(8,128)(2,1)}) %reduce-scatter.5.cloned.1.call-update) | async-done | bytes 65552 | tf_op jit(solution)/shard_map/reduce_scatter | solution.py:51
  529.8 1.5 convert_add_fusion
  531.3 92.4 %all-reduce.8.cloned.1.call-done = bf16[2,128,4096]{2,1,0:T(8,128)(2,1)} async-done(((bf16[2,128,4096]{2,1,0:T(8,128)(2,1)}), bf16[2,128,4096]{2,1,0:T(8,128)(2,1)}) %all-reduce.8.cloned.1.call-update) | async-done | bytes 2097168 | tf_op jit(solution)/shard_map/psum | solution.py:12
  623.7 5.0 fusion.22
  628.7 0.5 add_multiply_fusion
  (17 shorter events, 0.4 us)
Async XLA Ops:
  7.2 1.6 copy-start
  7.2 91.9 %reduce-scatter.3.cloned.1.call-start = ((), (), s32[]{:S(2)}) async-start(), calls=%async_computation.2 | async-start | bytes 4456448 | tf_op jit(solution)/shard_map/reduce_scatter | solution.py:35
  17.9 81.2 %copy-start.2 = (bf16[128,256]{1,0:T(8,128)(2,1)S(1)}, bf16[128,256]{1,0:T(8,128)(2,1)}, u32[]{:S(2)}) copy-start(bf16[128,256]{1,0:T(8,128)(2,1)} %param.10) | copy-start | bytes 196612
  18.0 126.2 %all-gather.4.cloned.1.call-start = ((), (), s32[]{:S(2)}) async-start(), calls=%async_computation.3 | async-start | bytes 1114112 | tf_op jit(solution)/shard_map/all_gather | solution.py:41
  100.8 94.0 %all-gather.6.cloned.1.call-start = ((), (), s32[]{:S(2)}) async-start(), calls=%async_computation.4 | async-start | bytes 9437184 | tf_op jit(solution)/shard_map/all_gather | solution.py:43
  101.5 144.7 %all-gather.8.cloned.1.call-start = ((), (), s32[]{:S(2)}) async-start(), calls=%async_computation.5 | async-start | bytes 9437184 | tf_op jit(solution)/shard_map/all_gather | solution.py:44
  102.1 247.9 %all-reduce.4.cloned.1.call-start = ((), (), s32[]{:S(2)}) async-start(), calls=%async_computation.7 | async-start | bytes 4194304 | tf_op jit(solution)/shard_map/psum | solution.py:12
  258.5 194.7 %all-reduce.6.cloned.1.call-start = ((), (), s32[]{:S(2)}) async-start(), calls=%async_computation.8 | async-start | bytes 4194304 | tf_op jit(solution)/shard_map/psum | solution.py:12
  362.3 167.5 %reduce-scatter.5.cloned.1.call-start = ((), (), s32[]{:S(2)}) async-start(), calls=%async_computation.6 | async-start | bytes 1114112 | tf_op jit(solution)/shard_map/reduce_scatter | solution.py:51
  369.8 160.0 %copy-start.1 = (bf16[128,256]{1,0:T(8,128)(2,1)S(1)}, bf16[128,256]{1,0:T(8,128)(2,1)}, u32[]{:S(2)}) copy-start(bf16[128,256]{1,0:T(8,128)(2,1)} %fusion.51) | copy-start | bytes 196612
  369.8 253.9 %all-reduce.8.cloned.1.call-start = ((), (), s32[]{:S(2)}) async-start(), calls=%async_computation.9 | async-start | bytes 4194304 | tf_op jit(solution)/shard_map/psum | solution.py:12
Sparse Core Ops, SparseCore 0:
  18.1 80.9 reduce-scatter.2
  101.8 42.3 all-gather.3
  145.9 48.9 all-gather.5
  196.4 49.8 all-gather.7
  258.6 91.4 all-reduce.3
  362.4 90.7 all-reduce.5
  456.3 73.3 reduce-scatter.4
  533.1 90.5 all-reduce.7
where the time goes:
time: 636 us
  waiting for transfers between devices  553 us (87%)
  matrix products  53.4 us (8%)
  between operations  14.2 us (2%)
  other arithmetic  8.67 us (1%)
    psum x3, waiting for transfers between devices, collect(): return lax.psum(partial_value.astype(jnp.bfloat16), 'tensor')  267 us
    reduce_scatter x1, waiting for transfers between devices, local(): lax.psum_scatter(partial_stats.reshape(batch_rows, 2, L), 'tensor', scatt...  81.1 us
    reduce_scatter x1, waiting for transfers between devices, local(): lax.psum_scatter(branch_part.astype(jnp.bfloat16), 'tensor', scatter_dime...  64.4 us
    all_gather x1, waiting for transfers between devices, local(): lax.all_gather(in_weight, 'dp', axis=0, tiled=True)  50.7 us
    all_gather x1, waiting for transfers between devices, local(): lax.all_gather(out_weight, 'dp', axis=0, tiled=True)  46.4 us
    all_gather x1, waiting for transfers between devices, local(): u_full = lax.all_gather(u_slice, 'tensor', axis=1, tiled=True)  42 us
    dot_general x3, matrix products, series(): jnp.einsum('pbh,lh->pbl', scaled, w_in, preferred_element_type=jnp.float32)  36.6 us
  transfers between devices with their start and end apart: 8, of which 8 were waited for; matrix products, arithmetic and copies ran while one was open for 4% of the time, Pallas kernels for 0%

commit v1 on v0

--- a/solution.py
+++ b/solution.py
@@ -39,9 +39,31 @@
         jnp.bfloat16
     )
     u_full = lax.all_gather(u_slice, "tensor", axis=1, tiled=True)
+
+    def report_levels_all(content, dim_i=0):
+        q_next, step_out, m_next = (lax.psum(1, "dp"), lax.axis_index("dp"), content.shape[dim_i])
+        so_far_all = [
+            dev_i * q_next if w == dim_i else dev_i for w, dev_i in enumerate(content.shape)
+        ]
+        kept_arr = lax.dynamic_update_slice_in_dim(
+            jnp.zeros(so_far_all, content.dtype), content, step_out * m_next, axis=dim_i
+        )
+        side_arr = passed = content
+        for u in range(1, q_next // 2 + 1):
+            side_arr = lax.ppermute(side_arr, "dp", [(w, (w + 1) % q_next) for w in range(q_next)])
+            kept_arr = lax.dynamic_update_slice_in_dim(
+                kept_arr, side_arr, (step_out - u) % q_next * m_next, axis=dim_i
+            )
+            if 2 * u < q_next:
+                passed = lax.ppermute(passed, "dp", [(w, (w - 1) % q_next) for w in range(q_next)])
+                kept_arr = lax.dynamic_update_slice_in_dim(
+                    kept_arr, passed, (step_out + u) % q_next * m_next, axis=dim_i
+                )
+        return kept_arr
+
     w_in, w_out = (
         lax.all_gather(in_weight, "dp", axis=0, tiled=True),
-        lax.all_gather(out_weight, "dp", axis=0, tiled=True),
+        report_levels_all(out_weight),
     )
     pre_act = jnp.dot(u_full, w_in, preferred_element_type=jnp.float32)
     tanh_val = jnp.tanh(pre_act)

time: 636 us -> 591 us (0.929)
  waiting for transfers between devices: 553 us -> 481 us
  local copies, waits for them, and re-layouts: 6.13 us -> 26.2 us
  starting transfers between devices: 0.5 us -> 7.43 us
    all_gather x1 -> x0, waiting for transfers between devices: 46.4 us -> none  [local(): lax.all_gather(out_weight, 'dp', axis=0, tiled=True)]
    ppermute x0 -> x7, waiting for transfers between devices: none -> 46.1 us  [the longest x4 46.1 us: report_levels_all(): lax.ppermute(side_arr, 'dp', [(w, (w + 1) % q_next) for w in range(q_next)])]
    all_gather x1, waiting for transfers between devices: 42 us -> 0.01 us  [local(): u_full = lax.all_gather(u_slice, 'tensor', axis=1, tiled=True)]
    all_gather x1, waiting for transfers between devices: 50.7 us -> 24.5 us  [local(): lax.all_gather(in_weight, 'dp', axis=0, tiled=True)]
    dynamic_update_slice x0 -> x8, local copies, waits for them, and re-layouts: none -> 13.5 us  [the longest x4 6.7 us: report_levels_all(): lax.dynamic_update_slice_in_dim(kept_arr, side_arr, (step_out - u) % q_ne...]
    ppermute x0 -> x7, starting transfers between devices: none -> 6.97 us  [the longest x3 6.94 us: report_levels_all(): lax.ppermute(passed, 'dp', [(w, (w - 1) % q_next) for w in range(q_next)])]
  transfers between devices with their start and end apart: 8 -> 14, of which waited for: 8 -> 10; matrix products, arithmetic and copies ran while one was open for 4% -> 7% of each run, Pallas kernels for 0% -> 0%
where the time goes in v1:
time: 591 us
  waiting for transfers between devices  481 us (81%)
  matrix products  53.6 us (9%)
  local copies, waits for them, and re-layouts  26.2 us (4%)
  between operations  14.2 us (2%)
  other arithmetic  8.67 us (1%)
  starting transfers between devices  7.43 us (1%)
    psum x3, waiting for transfers between devices, collect(): return lax.psum(partial_value.astype(jnp.bfloat16), 'tensor')  264 us
    reduce_scatter x1, waiting for transfers between devices, local(): lax.psum_scatter(partial_stats.reshape(batch_rows, 2, L), 'tensor', scatt...  81.1 us
    reduce_scatter x1, waiting for transfers between devices, local(): lax.psum_scatter(branch_part.astype(jnp.bfloat16), 'tensor', scatter_dime...  64.3 us
    ppermute x4, waiting for transfers between devices, report_levels_all(): lax.ppermute(side_arr, 'dp', [(w, (w + 1) % q_next) for w in range(q_next)])  46.1 us
    dot_general x3, matrix products, series(): jnp.einsum('pbh,lh->pbl', scaled, w_in, preferred_element_type=jnp.float32)  36.7 us
    all_gather x1, waiting for transfers between devices, local(): lax.all_gather(in_weight, 'dp', axis=0, tiled=True)  24.5 us
  transfers between devices with their start and end apart: 14, of which 10 were waited for; matrix products, arithmetic and copies ran while one was open for 7% of the time, Pallas kernels for 0%

profile of v1, /device:TPU:0, one launch (start us, length us, event | category | flops | bytes accessed | tf_op | source)
XLA Modules:
  0.0 590.6 jit_solution(2403640525030720859)
XLA Ops:
  8.8 4.6 fusion.55
  13.4 4.7 copy.12
  18.2 81.1 %reduce-scatter.3.cloned.1.call-done = f32[128,2,256]{2,0,1:T(8,128)} async-done(((f32[128,2,4096]{2,0,1:T(8,128)}), f32[128,2,256]{2,0,1:T(8,128)}) %reduce-scatter.3.cloned.1.call-update) | async-done | bytes 262160 | tf_op jit(solution)/shard_map/reduce_scatter | solution.py:35
  101.8 2.9 collective-permute-start.1
  104.7 12.5 %collective-permute-done = bf16[512,1024]{1,0:T(8,128)(2,1)S(1)} collective-permute-done((bf16[512,1024]{1,0:T(8,128)(2,1)S(1)}, bf16[512,1024]{1,0:T(8,128)(2,1)S(1)}, u32[]{:S(2)}, u32[]{:S(2)}) %collective-permute-start) | collective-permute-done | bytes 1048608 | tf_op jit(solution)/shard_map/ppermute | solution.py:53
  120.2 12.5 %collective-permute-done.2 = bf16[512,1024]{1,0:T(8,128)(2,1)S(1)} collective-permute-done((bf16[512,1024]{1,0:T(8,128)(2,1)S(1)}, bf16[512,1024]{1,0:T(8,128)(2,1)S(1)}, u32[]{:S(2)}, u32[]{:S(2)}) %collective-permute-start.2) | collective-permute-done | bytes 1048608 | tf_op jit(solution)/shard_map/ppermute | solution.py:53
  135.7 12.5 %collective-permute-done.4 = bf16[512,1024]{1,0:T(8,128)(2,1)} collective-permute-done((bf16[512,1024]{1,0:T(8,128)(2,1)S(1)}, bf16[512,1024]{1,0:T(8,128)(2,1)}, u32[]{:S(2)}, u32[]{:S(2)}) %collective-permute-start.4) | collective-permute-done | bytes 1048608 | tf_op jit(solution)/shard_map/ppermute | solution.py:53
  148.2 4.3 broadcast_in_dim.2
  156.8 2.4 constant_dynamic-update-slice_fusion.3
  159.2 2.3 constant_dynamic-update-slice_fusion.2
  161.4 2.3 constant_dynamic-update-slice_fusion.1
  163.7 8.7 %collective-permute-done.6 = bf16[512,1024]{1,0:T(8,128)(2,1)} collective-permute-done((bf16[512,1024]{1,0:T(8,128)(2,1)}, bf16[512,1024]{1,0:T(8,128)(2,1)}, u32[]{:S(2)}, u32[]{:S(2)}) %collective-permute-start.6) | collective-permute-done | bytes 1048608 | tf_op jit(solution)/shard_map/ppermute | solution.py:53
  172.4 2.3 constant_dynamic-update-slice_fusion
  174.8 24.5 %all-gather.5.cloned.1.call-done = bf16[4096,1024]{1,0:T(8,128)(2,1)} async-done(((bf16[512,1024]{1,0:T(8,128)(2,1)}), bf16[4096,1024]{1,0:T(8,128)(2,1)}) %all-gather.5.cloned.1.call-update) | async-done | bytes 8388624 | tf_op jit(solution)/shard_map/all_gather | solution.py:65
  199.3 5.0 multiply_subtract_fusion
  204.3 12.3 %fusion.12 = bf16[2,128,4096]{2,1,0:T(8,128)(2,1)} fusion(bf16[4096,1024]{1,0:T(8,128)(2,1)} %all-gather.5.cloned.1.call-done, bf16[2,128,4096]{2,1,0:T(8,128)(2,1)} %param.13, bf16[4096,1024]{1,0:T(8,128)(2,1)} %constant_dynamic-update-slice_fusion, f32[128,1024]{1,0:T(8,128)S(1)} %get-tuple-element.5), kind=kOutput, calls=%fused_computation.15 | convolution fusion | flops 4296540160 | bytes 21495808 | tf_op jit(solution)/shard_map/pbh,lh->pbl/dot_general | solution.py:22
  216.8 87.8 %all-reduce.4.cloned.1.call-done = bf16[2,128,4096]{2,1,0:T(8,128)(2,1)} async-done(((bf16[2,128,4096]{2,1,0:T(8,128)(2,1)}), bf16[2,128,4096]{2,1,0:T(8,128)(2,1)}) %all-reduce.4.cloned.1.call-update) | async-done | bytes 2097168 | tf_op jit(solution)/shard_map/psum | solution.py:12
  304.6 12.2 %fusion.15 = bf16[2,128,4096]{2,1,0:T(8,128)(2,1)} fusion(bf16[4096,1024]{1,0:T(8,128)(2,1)} %all-gather.5.cloned.1.call-done, bf16[2,128,4096]{2,1,0:T(8,128)(2,1)} %all-reduce.4.cloned.1.call-done, bf16[4096,1024]{1,0:T(8,128)(2,1)} %constant_dynamic-update-slice_fusion, f32[128,1024]{1,0:T(8,128)S(1)} %get-tuple-element.5), kind=kOutput, calls=%fused_computation.16 | convolution fusion | flops 4296540160 | bytes 21495808 | tf_op jit(solution)/shard_map/pbh,lh->pbl/dot_general | solution.py:22
  316.9 7.3 %convolution_convert_fusion = bf16[128,4096]{1,0:T(8,128)(2,1)} fusion(bf16[4096,1024]{1,0:T(8,128)(2,1)} %constant_dynamic-update-slice_fusion, bf16[128,1024]{1,0:T(8,128)(2,1)S(1)} %get-tuple-element.6), kind=kOutput, calls=%fused_computation.18 | convolution fusion | flops 1074266112 | bytes 9699328 | tf_op jit(solution)/shard_map/bh,lh->bl/dot_general | solution.py:72
  324.3 83.5 %all-reduce.6.cloned.1.call-done = bf16[2,128,4096]{2,1,0:T(8,128)(2,1)} async-done(((bf16[2,128,4096]{2,1,0:T(8,128)(2,1)}), bf16[2,128,4096]{2,1,0:T(8,128)(2,1)}) %all-reduce.6.cloned.1.call-update) | async-done | bytes 2097168 | tf_op jit(solution)/shard_map/psum | solution.py:12
  407.8 12.2 %fusion.18 = bf16[2,128,4096]{2,1,0:T(8,128)(2,1)} fusion(bf16[4096,1024]{1,0:T(8,128)(2,1)} %all-gather.5.cloned.1.call-done, bf16[2,128,4096]{2,1,0:T(8,128)(2,1)} %all-reduce.6.cloned.1.call-done, bf16[4096,1024]{1,0:T(8,128)(2,1)} %constant_dynamic-update-slice_fusion, f32[128,1024]{1,0:T(8,128)S(1)} %get-tuple-element.5), kind=kOutput, calls=%fused_computation.17 | convolution fusion | flops 4296540160 | bytes 21495808 | tf_op jit(solution)/shard_map/pbh,lh->pbl/dot_general | solution.py:22
  420.1 64.3 %reduce-scatter.5.cloned.1.call-done = bf16[128,256]{1,0:T(8,128)(2,1)} async-done(((bf16[128,4096]{1,0:T(8,128)(2,1)}), bf16[128,256]{1,0:T(8,128)(2,1)}) %reduce-scatter.5.cloned.1.call-update) | async-done | bytes 65552 | tf_op jit(solution)/shard_map/reduce_scatter | solution.py:73
  485.8 92.4 %all-reduce.8.cloned.1.call-done = bf16[2,128,4096]{2,1,0:T(8,128)(2,1)} async-done(((bf16[2,128,4096]{2,1,0:T(8,128)(2,1)}), bf16[2,128,4096]{2,1,0:T(8,128)(2,1)}) %all-reduce.8.cloned.1.call-update) | async-done | bytes 2097168 | tf_op jit(solution)/shard_map/psum | solution.py:12
  578.2 5.0 fusion.22
  (51 shorter events, 16.9 us)
Async XLA Ops:
  7.2 1.6 copy-start
  7.2 92.0 %reduce-scatter.3.cloned.1.call-start = ((), (), s32[]{:S(2)}) async-start(), calls=%async_computation.2 | async-start | bytes 4456448 | tf_op jit(solution)/shard_map/reduce_scatter | solution.py:35
  13.4 85.9 %copy-start.9 = (bf16[128,256]{1,0:T(8,128)(2,1)S(1)}, bf16[128,256]{1,0:T(8,128)(2,1)}, u32[]{:S(2)}) copy-start(bf16[128,256]{1,0:T(8,128)(2,1)} %param.10) | copy-start | bytes 196612
  13.4 88.4 %copy-start.1 = (bf16[512,1024]{1,0:T(8,128)(2,1)S(1)}, bf16[512,1024]{1,0:T(8,128)(2,1)}, u32[]{:S(2)}) copy-start(bf16[512,1024]{1,0:T(8,128)(2,1)} %param.12) | copy-start | bytes 3145732
  18.1 156.7 %all-gather.3.cloned.1.call-start = ((), (), s32[]{:S(2)}) async-start(), calls=%async_computation.3 | async-start | bytes 1114112 | tf_op jit(solution)/shard_map/all_gather | solution.py:41
  100.9 98.4 %all-gather.5.cloned.1.call-start = ((), (), s32[]{:S(2)}) async-start(), calls=%async_computation.4 | async-start | bytes 9437184 | tf_op jit(solution)/shard_map/all_gather | solution.py:65
  101.7 202.9 %all-reduce.4.cloned.1.call-start = ((), (), s32[]{:S(2)}) async-start(), calls=%async_computation.6 | async-start | bytes 4194304 | tf_op jit(solution)/shard_map/psum | solution.py:12
  101.7 15.4 %collective-permute-start = (bf16[512,1024]{1,0:T(8,128)(2,1)S(1)}, bf16[512,1024]{1,0:T(8,128)(2,1)S(1)}, u32[]{:S(2)}, u32[]{:S(2)}) collective-permute-start(bf16[512,1024]{1,0:T(8,128)(2,1)S(1)} %copy-done.1), channel_id=1, source_target_pairs={{0,16},{16,32},{32,48},{48,64},{64,80},{80,96},{96,112},{112,0},{1... | collective-permute-start | bytes 3145736 | tf_op jit(solution)/shard_map/ppermute | solution.py:53
  101.8 15.4 %collective-permute-start.1 = (bf16[512,1024]{1,0:T(8,128)(2,1)S(1)}, bf16[512,1024]{1,0:T(8,128)(2,1)S(1)}, u32[]{:S(2)}, u32[]{:S(2)}) collective-permute-start(bf16[512,1024]{1,0:T(8,128)(2,1)S(1)} %copy-done.1), channel_id=1, source_target_pairs={{0,112},{16,0},{32,16},{48,32},{64,48},{80,64},{96,80},{112,96},{1... | collective-permute-start | bytes 3145736 | tf_op jit(solution)/shard_map/ppermute | solution.py:58
  117.2 1.0 copy-start.2
  117.2 15.4 %collective-permute-start.2 = (bf16[512,1024]{1,0:T(8,128)(2,1)S(1)}, bf16[512,1024]{1,0:T(8,128)(2,1)S(1)}, u32[]{:S(2)}, u32[]{:S(2)}) collective-permute-start(bf16[512,1024]{1,0:T(8,128)(2,1)S(1)} %collective-permute-done), channel_id=1, source_target_pairs={{0,16},{16,32},{32,48},{48,64},{64,80},{80,96},{96,112},{112,0},{1... | collective-permute-start | bytes 3145736 | tf_op jit(solution)/shard_map/ppermute | solution.py:53
  118.2 14.4 %copy-start.4 = (bf16[512,1024]{1,0:T(8,128)(2,1)}, bf16[512,1024]{1,0:T(8,128)(2,1)S(1)}, u32[]{:S(2)}) copy-start(bf16[512,1024]{1,0:T(8,128)(2,1)S(1)} %collective-permute-done.1) | copy-start | bytes 3145732
  118.2 14.4 %collective-permute-start.3 = (bf16[512,1024]{1,0:T(8,128)(2,1)S(1)}, bf16[512,1024]{1,0:T(8,128)(2,1)}, u32[]{:S(2)}, u32[]{:S(2)}) collective-permute-start(bf16[512,1024]{1,0:T(8,128)(2,1)S(1)} %collective-permute-done.1), channel_id=1, source_target_pairs={{0,112},{16,0},{32,16},{48,32},{64,48},{80,64},{96,80},{112,96},{1... | collective-permute-start | bytes 3145736 | tf_op jit(solution)/shard_map/ppermute | solution.py:58
  132.6 1.0 copy-start.6
  132.6 15.5 %collective-permute-start.4 = (bf16[512,1024]{1,0:T(8,128)(2,1)S(1)}, bf16[512,1024]{1,0:T(8,128)(2,1)}, u32[]{:S(2)}, u32[]{:S(2)}) collective-permute-start(bf16[512,1024]{1,0:T(8,128)(2,1)S(1)} %collective-permute-done.2), channel_id=1, source_target_pairs={{0,16},{16,32},{32,48},{48,64},{64,80},{80,96},{96,112},{112,0},{1... | collective-permute-start | bytes 3145736 | tf_op jit(solution)/shard_map/ppermute | solution.py:53
  133.6 27.8 %collective-permute-start.5 = (bf16[512,1024]{1,0:T(8,128)(2,1)}, bf16[512,1024]{1,0:T(8,128)(2,1)}, u32[]{:S(2)}, u32[]{:S(2)}) collective-permute-start(bf16[512,1024]{1,0:T(8,128)(2,1)} %collective-permute-done.3), channel_id=1, source_target_pairs={{0,112},{16,0},{32,16},{48,32},{64,48},{80,64},{96,80},{112,96},{1... | collective-permute-start | bytes 3145736 | tf_op jit(solution)/shard_map/ppermute | solution.py:58
  148.2 24.3 %collective-permute-start.6 = (bf16[512,1024]{1,0:T(8,128)(2,1)}, bf16[512,1024]{1,0:T(8,128)(2,1)}, u32[]{:S(2)}, u32[]{:S(2)}) collective-permute-start(bf16[512,1024]{1,0:T(8,128)(2,1)} %collective-permute-done.4), channel_id=1, source_target_pairs={{0,16},{16,32},{32,48},{48,64},{64,80},{80,96},{96,112},{112,0},{1... | collective-permute-start | bytes 3145736 | tf_op jit(solution)/shard_map/ppermute | solution.py:53
  148.2 5.5 copy-start.3
  148.2 6.5 %copy-start.5 = (bf16[512,1024]{1,0:T(8,128)(2,1)S(1)}, bf16[512,1024]{1,0:T(8,128)(2,1)}, u32[]{:S(2)}) copy-start(bf16[512,1024]{1,0:T(8,128)(2,1)} %copy-done.4) | copy-start | bytes 3145732
  148.2 7.6 %copy-start.7 = (bf16[512,1024]{1,0:T(8,128)(2,1)S(1)}, bf16[512,1024]{1,0:T(8,128)(2,1)}, u32[]{:S(2)}) copy-start(bf16[512,1024]{1,0:T(8,128)(2,1)} %copy-done.6) | copy-start | bytes 3145732
  216.6 191.2 %all-reduce.6.cloned.1.call-start = ((), (), s32[]{:S(2)}) async-start(), calls=%async_computation.7 | async-start | bytes 4194304 | tf_op jit(solution)/shard_map/psum | solution.py:12
  316.9 167.5 %reduce-scatter.5.cloned.1.call-start = ((), (), s32[]{:S(2)}) async-start(), calls=%async_computation.5 | async-start | bytes 1114112 | tf_op jit(solution)/shard_map/reduce_scatter | solution.py:73
  324.2 160.1 %copy-start.8 = (bf16[128,256]{1,0:T(8,128)(2,1)S(1)}, bf16[128,256]{1,0:T(8,128)(2,1)}, u32[]{:S(2)}) copy-start(bf16[128,256]{1,0:T(8,128)(2,1)} %fusion.54) | copy-start | bytes 196612
  324.2 254.0 %all-reduce.8.cloned.1.call-start = ((), (), s32[]{:S(2)}) async-start(), calls=%async_computation.8 | async-start | bytes 4194304 | tf_op jit(solution)/shard_map/psum | solution.py:12
Sparse Core Ops, SparseCore 0:
  18.2 80.9 reduce-scatter.2
  101.9 42.3 all-gather.2
  146.0 53.2 all-gather.4
  216.7 87.8 all-reduce.3
  317.0 90.7 all-reduce.5
  410.9 73.4 reduce-scatter.4
  487.7 90.5 all-reduce.7
